TPU v7x, 128 devices: a whole 4x4x4 slice. The times are simulated.
128 devices in a mesh: valve: 8 (over y, core), bulk: 16 (over z, x).
Axes of the slice: x: 4, y: 4, z: 4, core: 2. Of those that a mesh axis runs over, the one named last changes fastest.
Arguments:
- solution: float32 [5, 64, 131072], P(None, None, ('valve', 'bulk')), may hold values from -6 to 6
- velocity: float32 [3, 131072], P(None, ('valve', 'bulk')), may hold values from -1 to 1
- inv_jacobian: float32 [64, 131072], P(None, ('valve', 'bulk')), may hold values from 0.5 to 3
- face_speed: float32 [96, 131072], P(None, ('valve', 'bulk')), may hold values from -6 to 6
- face_link: int32 [6, 131072], P(None, ('valve', 'bulk')), may hold values from 0 to 6271, as said below
- donor_elem: int32 [1048576], P(('valve', 'bulk')), may hold values from 0 to 1023
- ref_coords: float32 [3, 1048576], P(None, ('valve', 'bulk')), may hold values from -1 to 1
- owner_list: int32 [1048576, 1], P(('valve', 'bulk')), may hold values from 0 to 15; in each aligned block of 8192 rows (0 to 8191, 8192 to 16383, ...) at most 1024 rows name the same one
Outputs:
- section_rate: float32 [5, 64, 131072], P(None, None, ('valve', 'bulk'))
- fringe_values: float32 [5, 2097152], P(None, ('valve', 'bulk'))
Inputs may be any that keep to these rules, and one draw needn't show every extreme that they name: `face_link`: on each device, the values 6 * 1024 to 6271 appear exactly once each; every other face slot links to another slot of the same device that links back to it. `owner_list`: among the receptors of one device no owner is named more than 1024 times; in every draw some device names some owner exactly 1024 times.
All inputs are finite; a program needn't handle non-finite values.
Results may differ from a plain program's by a relative error of at most 0.0003.
Values sent between devices are 32-bit elements; how exact they have to be, the bound alone decides.
No kernel may reach another device: no remote copies, remote signals or barrier semaphores. Data moves between devices by JAX's collectives and lax.ppermute only.
A program may use at most 192 MiB of HBM per device.

v0:
```python
import jax
import jax.numpy as jnp
import numpy as np
from jax import lax
from jax.sharding import PartitionSpec as P

gauss_nodes = (-0.8611363115940526, -0.3399810435848563, 0.3399810435848563, 0.8611363115940526)
quad_weights = (0.3478548451374538, 0.6521451548625461, 0.6521451548625461, 0.3478548451374538)
section_step = 0.2


def padded(shard, sides, width):
    for axis, dim in sides:
        size, length = (lax.axis_size(axis), shard.shape[dim])
        up = [(i, (i + 1) % size) for i in range(size)]
        down = [(j, i) for i, j in up]
        last = lax.slice_in_dim(shard, length - width, length, axis=dim)
        initial = lax.slice_in_dim(shard, 0, width, axis=dim)
        before = lax.ppermute(last, axis, up)
        after = lax.ppermute(initial, axis, down)
        shard = jnp.concatenate([before, shard, after], axis=dim)
    return shard


def lagrange_at(x):
    values = []
    for j in range(4):
        factor = 1.0
        for m in range(4):
            if m != j:
                factor = factor * (x - gauss_nodes[m]) / (gauss_nodes[j] - gauss_nodes[m])
        values.append(factor)
    return values


def tables():
    slopes = np.zeros((4, 4))
    for i in range(4):
        for j in range(4):
            summed = 0.0
            for m in range(4):
                if m != j:
                    product = 1.0 / (gauss_nodes[j] - gauss_nodes[m])
                    for n in range(4):
                        if n != j and n != m:
                            product = (
                                product
                                * (gauss_nodes[i] - gauss_nodes[n])
                                / (gauss_nodes[j] - gauss_nodes[n])
                            )
                    summed = summed + product
            slopes[i, j] = summed
    end_values = [lagrange_at(-1.0), lagrange_at(1.0)]
    extrapolate = np.zeros((96, 64))
    lifting = np.zeros((64, 96))
    derivative = np.zeros((3, 64, 64))
    for p in range(64):
        point_idx = (p // 16, p // 4 % 4, p % 4)
        for f in range(6):
            normal_dir = f // 2
            across = [t for t in range(3) if t != normal_dir]
            q = point_idx[across[0]] * 4 + point_idx[across[1]]
            flux_row = q * 6 + f
            extrapolate[flux_row, p] = end_values[f % 2][point_idx[normal_dir]]
            lifting[p, flux_row] = (
                end_values[f % 2][point_idx[normal_dir]] / quad_weights[point_idx[normal_dir]]
            )
        for s in range(64):
            other_idx = (s // 16, s // 4 % 4, s % 4)
            for normal_dir in range(3):
                if all((point_idx[t] == other_idx[t] for t in range(3) if t != normal_dir)):
                    derivative[normal_dir, p, s] = slopes[
                        point_idx[normal_dir], other_idx[normal_dir]
                    ]
    return (
        jnp.asarray(extrapolate, dtype=jnp.float32),
        jnp.asarray(derivative, dtype=jnp.float32),
        jnp.asarray(lifting, dtype=jnp.float32),
    )


def face_rows(solution, face_speed, extrapolate):
    nvars = solution.shape[0]
    elems = solution.shape[2]
    ext_faces = extrapolate.reshape(16, 6, 64)
    values = jnp.einsum("qfp,vpe->feqv", ext_faces, solution, precision=lax.Precision.HIGHEST)
    values = values.reshape(6 * elems, 16, nvars)
    speeds = jnp.transpose(face_speed.reshape(16, 6, elems), (1, 2, 0)).reshape(6 * elems, 16)
    return (values, speeds)


def rim_rows(table_own, links, faces_total, rim_count):
    slots = jnp.where(links >= faces_total, links - faces_total, 2 * rim_count)
    senders = (
        jnp.zeros((2 * rim_count,), jnp.int32)
        .at[slots]
        .set(jnp.arange(faces_total, dtype=jnp.int32), mode="drop")
    )
    return jnp.take(table_own, senders, axis=0)


def surface_term(values, speeds, table_own, links, received, lifting, elems):
    nvars = values.shape[2]
    full_table = jnp.concatenate([table_own, received], axis=0)
    outer = jnp.take(full_table, links, axis=0)
    outer_vals = outer[:, : 16 * nvars].reshape(6 * elems, 16, nvars)
    outer_speed = outer[:, 16 * nvars :][:, :, None]
    own_speed = speeds[:, :, None]
    normal = 0.5 * (own_speed - outer_speed)
    common = 0.5 * normal * (values + outer_vals) + 0.5 * jnp.abs(normal) * (values - outer_vals)
    jump_term = (common - own_speed * values).reshape(6, elems, 16, nvars)
    lift_faces = lifting.reshape(64, 16, 6)
    return jnp.einsum("pqf,feqv->vpe", lift_faces, jump_term, precision=lax.Precision.HIGHEST)


def volume_term(solution, velocity, derivative):
    slopes = jnp.einsum("dpq,vqe->dvpe", derivative, solution, precision=lax.Precision.HIGHEST)
    return jnp.sum(velocity[:, None, None, :] * slopes, axis=0)


def receptor_rows(advanced, donors, coords):
    nvars = advanced.shape[0]
    elems = advanced.shape[2]
    basis_x = jnp.stack(lagrange_at(coords[0]))
    basis_y = jnp.stack(lagrange_at(coords[1]))
    basis_z = jnp.stack(lagrange_at(coords[2]))
    weights = (
        basis_x[:, None, None, :] * basis_y[None, :, None, :] * basis_z[None, None, :, :]
    ).reshape(64, -1)
    element_rows = jnp.transpose(advanced, (2, 0, 1)).reshape(elems, nvars * 64)
    picked = jnp.take(element_rows, donors, axis=0).reshape(donors.shape[0], nvars, 64)
    return jnp.einsum("rvp,pr->rv", picked, weights, precision=lax.Precision.HIGHEST)


def on_device(
    solution, velocity, inv_jacobian, face_speed, face_link, donor_elem, ref_coords, owner_list
):
    extrapolate, derivative, lifting = tables()
    nvars = solution.shape[0]
    elems = solution.shape[2]
    rim_count = elems // 16
    faces_total = 6 * elems
    links = face_link.reshape(faces_total)
    values, speeds = face_rows(solution, face_speed, extrapolate)
    table_own = jnp.concatenate([values.reshape(faces_total, 16 * nvars), speeds], axis=1)
    outgoing = rim_rows(table_own, links, faces_total, rim_count)
    extended = padded(outgoing, (("valve", 0),), rim_count)
    received = jnp.concatenate([extended[:rim_count], extended[3 * rim_count :]], axis=0)
    surface = surface_term(values, speeds, table_own, links, received, lifting, elems)
    volume = volume_term(solution, velocity, derivative)
    section_rate = -inv_jacobian[None] * (volume + surface)
    advanced = solution + section_step * section_rate
    receptor_vals = receptor_rows(advanced, donor_elem, ref_coords)
    buckets = lax.axis_size("bulk")
    receptors = receptor_vals.shape[0]
    capacity = 2 * receptors // buckets
    owners = owner_list[:, 0]
    gathered_vals, gathered_owners = (
        lax.all_gather(receptor_vals, "bulk", axis=0, tiled=True),
        lax.all_gather(owners, "bulk", axis=0, tiled=True),
    )
    by_source = gathered_owners.reshape(buckets, receptors)
    matches = (by_source == lax.axis_index("bulk")).astype(jnp.int32)
    before = jnp.cumsum(matches, axis=1) - matches
    places = jnp.where(
        matches == 1,
        jnp.arange(buckets, dtype=jnp.int32)[:, None] * capacity + before,
        buckets * capacity,
    ).reshape(buckets * receptors)
    fringe_rows = jnp.zeros((buckets * capacity, nvars), jnp.float32)
    fringe_rows = fringe_rows.at[places].set(gathered_vals, mode="drop")
    return (section_rate, jnp.transpose(fringe_rows))


def solution(mesh):
    placed = (
        P(None, None, ("valve", "bulk")),
        P(None, ("valve", "bulk")),
        P(None, ("valve", "bulk")),
        P(None, ("valve", "bulk")),
        P(None, ("valve", "bulk")),
        P(("valve", "bulk")),
        P(None, ("valve", "bulk")),
        P(("valve", "bulk"), None),
    )
    return jax.shard_map(
        on_device,
        mesh=mesh,
        in_specs=placed,
        out_specs=(P(None, None, ("valve", "bulk")), P(None, ("valve", "bulk"))),
        check_vma=False,
    )
```

profile of v0, /device:TPU:9, one launch (start us, length us, event | category | flops | bytes accessed | tf_op | source)
XLA Modules:
  0.0 904.9 jit_solution(7143843174503303031)
XLA Ops:
  7.2 0.0 copy-start.14
  7.2 0.0 all-gather.3.cloned.1.call-start
  7.2 0.8 copy.45
  8.0 0.1 compare_select_fusion.1
  8.1 23.0 %scatter_custom_fusion = s32[128]{0:T(128)S(1)} fusion(s32[6144]{0:T(1024)S(1)} %bitcast.87, s32[6144]{0:T(1024)S(1)} %iota.8, s32[]{:T(128)} %constant.125.clone.1), kind=kCustom, calls=%fused_computation.82 | custom fusion | bytes 516 | tf_op jit(solution)/shard_map/scatter | solution.py:97
  31.1 1.8 reshape.165
  33.0 1.9 copy.19
  34.9 4.0 convolution_bitcast_fusion
  38.9 1.2 copy.20
  40.1 2.5 copy.44
  42.6 3.4 copy.21
  46.0 0.0 copy-start.13
  46.0 0.0 copy-start.12
  46.0 0.0 copy-start.17
  46.1 4.6 pad_maximum_fusion.1
  50.6 2.6 gather_fusion
  53.2 0.1 broadcast_select_fusion.1
  53.3 1.9 collective-permute-start
  55.2 0.0 collective-permute-start.1
  55.3 0.6 fusion.25
  55.9 0.0 copy-done.13
  55.9 0.8 multiply_multiply_fusion.11
  56.7 0.2 pad_maximum_fusion.2
  57.0 0.0 copy-start.16
  57.0 0.1 broadcast_multiply_fusion.2
  57.1 0.0 copy-done.12
  57.1 0.0 copy-start.7
  57.1 0.0 copy-start.9
  57.1 4.4 multiply_reduce_fusion.1
  61.5 0.1 pad_maximum_fusion.4
  61.6 0.5 broadcast_multiply_fusion.1
  62.2 22.1 %all-gather = s32[131072,1]{0,1:T(1,128)} all-gather(s32[8192,1]{0,1:T(1,128)S(1)} %copy-done.16), channel_id=2, replica_groups=mesh['valve'=8,'bulk'=16] {'bulk'}, dimensions={0}, use_global_device_ids=true | all-gather | bytes 557056 | tf_op jit(solution)/shard_map/all_gather | solution.py:160
  84.2 1.0 copy.27
  85.2 2.0 mul.255
  87.2 0.0 collective-permute-done
  87.2 0.6 copy-done.15
  87.8 0.0 collective-permute-done.1
  87.8 3.8 pad_maximum_fusion
  91.6 21.1 %gather_fusion.1 = f32[6144,96]{1,0:T(8,128)} fusion(f32[6272,96]{1,0:T(8,128)S(1)} %pad_maximum_fusion, s32[6144]{0:T(1024)S(1)} %broadcast_clamp_fusion), kind=kCustom, calls=%fused_computation.1 | custom fusion | bytes 4743168 | tf_op jit(solution)/shard_map/jit(_take)/gather | solution.py:105
  112.6 4.8 broadcast_select_fusion
  117.5 3.5 broadcast_multiply_fusion
  120.9 2.2 copy.23
  123.1 3.4 reshape.169
  126.5 3.2 copy.22
  129.6 3.0 copy.25
  132.6 7.4 multiply_add_fusion
  140.1 1.8 copy.29
  141.9 34.8 %gather_fusion.2 = f32[8192,320]{1,0:T(8,128)} fusion(f32[1024,320]{1,0:T(8,128)S(1)} %copy.29, s32[8192]{0:T(1024)} %fusion.25), kind=kCustom, calls=%fused_computation.2 | custom fusion | bytes 21004288 | tf_op jit(solution)/shard_map/jit(_take)/gather | solution.py:131
  176.7 12.1 %copy.30 = f32[8192,320]{0,1:T(8,128)} copy(f32[8192,320]{1,0:T(8,128)} %gather_fusion.2) | data formatting | bytes 20971520 | tf_op jit(solution)/shard_map/jit(_take)/gather | solution.py:131
  188.8 5.7 multiply_reduce_fusion
  194.4 2.7 copy.42
  197.1 0.0 all-gather.3.cloned.1.call-update
  197.2 1.0 copy-done.8
  198.2 0.5 compare_convert_fusion
  198.7 0.1 broadcast_bitcast_fusion
  198.8 0.1 copy.46
  198.9 5.0 reduce-window.6
  203.9 0.5 slice_reduce_fusion
  204.4 0.2 reduce-window.9
  204.6 0.2 broadcast_add_fusion
  204.8 0.1 compare_select_fusion
  204.9 365.3 %all-gather.3.cloned.1.call-done = f32[131072,5]{1,0:T(8,128)} async-done(((f32[8192,5]{1,0:T(8,128)}), f32[131072,5]{1,0:T(8,128)}) %all-gather.3.cloned.1.call-update) | async-done | bytes 2621456 | tf_op jit(solution)/shard_map/all_gather | solution.py:159
  570.2 321.9 %scatter_custom_fusion.1 = f32[16384,5]{1,0:T(8,128)} fusion(s32[131072]{0:T(1024)S(1)} %compare_select_fusion, f32[131072,5]{1,0:T(8,128)} %all-gather.3.cloned.1.call-done, f32[]{:T(128)} %constant.124.clone.1), kind=kCustom, calls=%fused_computation.6 | custom fusion | bytes 328192 | tf_op jit(solution)/shard_map/scatter | solution.py:171
  892.1 6.0 copy.31
  (36 shorter events, 0.1 us)
Async XLA Ops:
  7.2 27.7 %copy-start.14 = (f32[16,6,64,1]{2,0,3,1:T(8,128)S(1)}, f32[16,6,64,1]{2,0,3,1:T(8,128)}, u32[]{:S(2)}) copy-start(f32[16,6,64,1]{2,0,3,1:T(8,128)} %constant.160) | copy-start | bytes 73732
  7.2 563.0 %all-gather.3.cloned.1.call-start = ((), (), s32[]{:S(2)}) async-start(), calls=%async_computation | async-start | bytes 71303168 | tf_op jit(solution)/shard_map/all_gather | solution.py:159
  34.9 11.1 %copy-start = (f32[6,1024,16]{2,1,0:T(8,128)}, f32[6,1024,16]{2,1,0:T(8,128)S(1)}, u32[]{:S(2)}) copy-start(f32[6,1024,16]{2,1,0:T(8,128)S(1)} %copy.19) | copy-start | bytes 1179652
  38.9 3.7 copy-start.2
  46.0 9.2 %copy-start.10 = (s32[6,1024]{1,0:T(8,128)S(1)}, s32[6,1024]{1,0:T(8,128)}, u32[]{:S(2)}) copy-start(s32[6,1024]{1,0:T(8,128)} %param.15) | copy-start | bytes 73732
  46.0 9.2 %copy-start.11 = (s32[8192]{0:T(1024)S(1)}, s32[8192]{0:T(1024)}, u32[]{:S(2)}) copy-start(s32[8192]{0:T(1024)} %param.16) | copy-start | bytes 98308
  46.0 9.9 %copy-start.13 = (f32[3,8192]{1,0:T(4,128)S(1)}, f32[3,8192]{1,0:T(4,128)}, u32[]{:S(2)}) copy-start(f32[3,8192]{1,0:T(4,128)} %param.17) | copy-start | bytes 294916
  46.0 11.1 %copy-start.12 = (f32[3,64,64,1]{2,1,3,0:T(8,128)S(1)}, f32[3,64,64,1]{2,1,3,0:T(8,128)}, u32[]{:S(2)}) copy-start(f32[3,64,64,1]{2,1,3,0:T(8,128)} %constant.159) | copy-start | bytes 147460
  46.0 11.1 %copy-start.17 = (f32[3,1024]{1,0:T(4,128)S(1)}, f32[3,1024]{1,0:T(4,128)}, u32[]{:S(2)}) copy-start(f32[3,1024]{1,0:T(4,128)} %param.12) | copy-start | bytes 36868
  50.6 6.5 copy-start.4
  53.3 33.8 %collective-permute-start = (f32[64,96]{1,0:T(8,128)S(1)}, f32[64,96]{1,0:T(8,128)S(1)}, u32[]{:S(2)}, u32[]{:S(2)}) collective-permute-start(f32[64,96]{1,0:T(8,128)S(1)} %get-tuple-element.18), channel_id=1, source_target_pairs={{0,16},{16,32},{32,48},{48,64},{64,80},{80,96},{96,112},{112,0},{1... | collective-permute-start | bytes 73736 | tf_op jit(solution)/shard_map/ppermute | solution.py:19
  55.2 32.6 %collective-permute-start.1 = (f32[64,96]{1,0:T(8,128)S(1)}, f32[64,96]{1,0:T(8,128)}, u32[]{:S(2)}, u32[]{:S(2)}) collective-permute-start(f32[64,96]{1,0:T(8,128)S(1)} %get-tuple-element.19), channel_id=1, source_target_pairs={{16,0},{32,16},{48,32},{64,48},{80,64},{96,80},{112,96},{0,112},{1... | collective-permute-start | bytes 73736 | tf_op jit(solution)/shard_map/ppermute | solution.py:20
  57.0 5.2 copy-start.16
  57.1 27.1 %copy-start.7 = (f32[16,6,1024]{2,1,0:T(8,128)S(1)}, f32[16,6,1024]{2,1,0:T(8,128)}, u32[]{:S(2)}) copy-start(f32[16,6,1024]{2,1,0:T(8,128)} %reshape.165) | copy-start | bytes 1179652
  57.1 28.1 %copy-start.9 = (f32[64,1024]{1,0:T(8,128)S(1)}, f32[64,1024]{1,0:T(8,128)}, u32[]{:S(2)}) copy-start(f32[64,1024]{1,0:T(8,128)} %param.13) | copy-start | bytes 786436
  87.2 0.6 copy-start.15
  112.6 4.8 copy-start.1
  126.5 6.2 copy-start.3
  126.5 6.2 copy-start.5
  176.7 12.1 %copy-start.6 = (f32[64,8192]{1,0:T(8,128)S(1)}, f32[64,8192]{1,0:T(8,128)}, u32[]{:S(2)}) copy-start(f32[64,8192]{1,0:T(8,128)} %mul.255) | copy-start | bytes 6291460
  197.1 1.0 copy-start.8
Sparse Core Ops, SparseCore 0:
  197.3 372.8 all-gather.2
where the time goes:
time: 907 us; the launch traced here: 905 us
  local copies, waits for them, and re-layouts  455 us (50%)
  waiting for transfers between devices  365 us (40%)
  other arithmetic  30.8 us (3%)
  blocking collectives  22.1 us (2%)
  matrix products  15.8 us (2%)
  between operations  14.4 us (2%)
    all_gather x1, waiting for transfers between devices, on_device(): lax.all_gather(receptor_vals, 'bulk', axis=0, tiled=True)  365 us
    scatter x1, local copies, waits for them, and re-layouts, on_device(): fringe_rows = fringe_rows.at[places].set(gathered_vals, mode='drop')  322 us
    gather x2, local copies, waits for them, and re-layouts, receptor_rows(): jnp.take(element_rows, donors, axis=0).reshape(donors.shape[0], nvars, 64)  46.9 us
    scatter x1, local copies, waits for them, and re-layouts, rim_rows(): senders = jnp.zeros((2 * rim_count,), jnp.int32).at[slots].set(jnp.arange...  23 us
    all_gather x1, blocking collectives, on_device(): lax.all_gather(owners, 'bulk', axis=0, tiled=True)  22.1 us
    gather x1, local copies, waits for them, and re-layouts, surface_term(): outer = jnp.take(full_table, links, axis=0)  21.1 us
  transfers between devices with their start and end apart: 3, of which 1 were waited for; matrix products, arithmetic and copies ran while one was open for 2% of the time, Pallas kernels for 0%

commit v1 on v0

--- a/solution.py
+++ b/solution.py
@@ -155,21 +155,16 @@
     receptors = receptor_vals.shape[0]
     capacity = 2 * receptors // buckets
     owners = owner_list[:, 0]
-    gathered_vals, gathered_owners = (
-        lax.all_gather(receptor_vals, "bulk", axis=0, tiled=True),
-        lax.all_gather(owners, "bulk", axis=0, tiled=True),
-    )
-    by_source = gathered_owners.reshape(buckets, receptors)
-    matches = (by_source == lax.axis_index("bulk")).astype(jnp.int32)
-    before = jnp.cumsum(matches, axis=1) - matches
-    places = jnp.where(
-        matches == 1,
-        jnp.arange(buckets, dtype=jnp.int32)[:, None] * capacity + before,
-        buckets * capacity,
-    ).reshape(buckets * receptors)
-    fringe_rows = jnp.zeros((buckets * capacity, nvars), jnp.float32)
-    fringe_rows = fringe_rows.at[places].set(gathered_vals, mode="drop")
-    return (section_rate, jnp.transpose(fringe_rows))
+    onehot = (owners[:, None] == jnp.arange(buckets, dtype=jnp.int32)[None, :]).astype(jnp.int32)
+    before = jnp.cumsum(onehot, axis=0) - onehot
+    ranks = jnp.sum(before * onehot, axis=1)
+    places = owners * capacity + ranks
+    send = jnp.zeros((buckets * capacity, nvars), jnp.float32)
+    send = send.at[places].set(receptor_vals, mode="drop", unique_indices=True)
+    send = jnp.transpose(send.reshape(buckets, capacity, nvars), (0, 2, 1))
+    got = lax.all_to_all(send, "bulk", 0, 0, tiled=True)
+    fringe = jnp.transpose(got, (1, 0, 2)).reshape(nvars, buckets * capacity)
+    return (section_rate, fringe)
 
 
 def solution(mesh):

time: 907 us -> 226 us (0.25)
  waiting for transfers between devices: 365 us -> 0.01 us
  local copies, waits for them, and re-layouts: 455 us -> 155 us
  between operations: 14.4 us -> 0.97 us
    all_gather x1 -> x0, waiting for transfers between devices: 365 us -> none  [on_device(): lax.all_gather(receptor_vals, 'bulk', axis=0, tiled=True)]
    scatter x1, local copies, waits for them, and re-layouts: 322 us -> 24.5 us  [on_device(): send = send.at[places].set(receptor_vals, mode='drop', unique_indices=True)]
    all_gather x1 -> x0, blocking collectives: 22.1 us -> none  [on_device(): lax.all_gather(owners, 'bulk', axis=0, tiled=True)]
    all_to_all x0 -> x1, blocking collectives: none -> 19.8 us  [on_device(): got = lax.all_to_all(send, 'bulk', 0, 0, tiled=True)]
  transfers between devices with their start and end apart: 3 -> 2, of which waited for: 1 -> 0; matrix products, arithmetic and copies ran while one was open for 2% -> 7% of each run, Pallas kernels for 0% -> 0%
where the time goes in v1:
time: 226 us; the launch traced here: 225 us
  local copies, waits for them, and re-layouts  155 us (69%)
  other arithmetic  31.3 us (14%)
  blocking collectives  19.8 us (9%)
  matrix products  15.7 us (7%)
    gather x2, local copies, waits for them, and re-layouts, receptor_rows(): jnp.take(element_rows, donors, axis=0).reshape(donors.shape[0], nvars, 64)  46.7 us
    scatter x1, local copies, waits for them, and re-layouts, on_device(): send = send.at[places].set(receptor_vals, mode='drop', unique_indices=True)  24.5 us
    scatter x1, local copies, waits for them, and re-layouts, rim_rows(): senders = jnp.zeros((2 * rim_count,), jnp.int32).at[slots].set(jnp.arange...  23 us
    gather x1, local copies, waits for them, and re-layouts, surface_term(): outer = jnp.take(full_table, links, axis=0)  20.9 us
    all_to_all x1, blocking collectives, on_device(): got = lax.all_to_all(send, 'bulk', 0, 0, tiled=True)  19.8 us
    dot_general x1, matrix products, surface_term(): jnp.einsum('pqf,feqv->vpe', lift_faces, jump_term, precision=lax.Precisio...  7.39 us
    unnamed x1, other arithmetic  5.69 us
    another operation x3, other arithmetic  5.35 us
  transfers between devices with their start and end apart: 2, of which 0 were waited for; matrix products, arithmetic and copies ran while one was open for 7% of the time, Pallas kernels for 0%

profile of v1, /device:TPU:9, one launch (start us, length us, event | category | flops | bytes accessed | tf_op | source)
XLA Modules:
  0.0 225.0 jit_solution(4338625363912888678)
XLA Ops:
  0.6 0.0 copy-start.14
  0.6 0.8 copy.56
  1.4 0.1 compare_select_fusion.1
  1.5 23.0 %scatter_custom_fusion = s32[128]{0:T(128)S(1)} fusion(s32[6144]{0:T(1024)S(1)} %bitcast.107, s32[6144]{0:T(1024)S(1)} %iota.11, s32[]{:T(128)} %constant.122.clone.1), kind=kCustom, calls=%fused_computation.86 | custom fusion | bytes 516 | tf_op jit(solution)/shard_map/scatter | solution.py:97
  24.5 1.8 reshape.164
  26.4 1.9 copy.32
  28.3 0.0 copy-done.14
  28.3 0.0 copy-start
  28.3 4.0 %convolution_bitcast_fusion = f32[6,1024,16,5]{1,2,3,0:T(8,128)S(1)} fusion(f32[16,6,64,1]{2,0,3,1:T(8,128)S(1)} %copy-done.14, f32[5,64,1024]{2,1,0:T(8,128)} %param.11), kind=kOutput, calls=%fused_computation.22 | convolution fusion | flops 377487360 | bytes 3301376 | tf_op jit(solution)/shard_map/qfp,vpe->feqv/dot_general | solution.py:86
  32.3 1.2 copy.33
  33.5 2.5 %copy.55 = f32[10,8,6,1024]{3,1,2,0:T(8,128)} copy(f32[10,8,6,1024]{3,2,1,0:T(8,128)S(1)} %bitcast.90) | data formatting | bytes 3932160
  36.1 3.3 %copy.34 = f32[6144,80]{1,0:T(8,128)} copy(f32[6144,80]{0,1:T(8,128)} %bitcast.92) | data formatting | bytes 3932160 | tf_op jit(solution)/shard_map/reshape;reshape | solution.py:145
  39.4 0.0 copy-start.10
  39.4 0.0 copy-start.11
  39.4 0.0 copy-start.8
  39.4 4.5 %pad_maximum_fusion.1 = f32[6144,96]{1,0:T(8,128)} fusion(f32[6144,16]{1,0:T(8,128)S(1)} %bitcast.83, f32[6144,80]{1,0:T(8,128)} %copy.34), kind=kLoop, calls=%fused_computation.11 | loop fusion | flops 589824 | bytes 4718592 | tf_op jit(solution)/shard_map/concatenate | solution.py:145
  43.9 2.6 %gather_fusion = f32[128,96]{1,0:T(8,128)S(1)} fusion(f32[6144,96]{1,0:T(8,128)} %pad_maximum_fusion.1, s32[1024]{0:T(1024)S(1)} %pad_clamp_fusion), kind=kCustom, calls=%fused_computation | custom fusion | bytes 98816 | tf_op jit(solution)/shard_map/jit(_take)/gather | solution.py:99
  46.5 0.1 broadcast_select_fusion.1
  46.6 0.7 collective-permute-start.1
  47.3 1.2 collective-permute-start
  48.5 0.0 copy-done.11
  48.5 0.6 fusion.29
  49.2 0.0 copy-done.8
  49.2 4.9 %reduce-window.6 = s32[16,64,128]{2,1,0:T(8,128)S(1)} reduce-window(s32[16,64,128]{2,1,0:T(8,128)S(1)} %fusion.28, s32[]{:T(128)} %constant.122.clone.1), window={size=1x1x128 pad=0_0x0_0x127_0}, to_apply=%region_2.3 | reduce-window | flops 16646144 | bytes 1048580 | tf_op jit(solution)/shard_map/reduce-window
  54.2 0.5 slice_reduce_fusion
  54.7 0.2 reduce-window.9
  54.9 0.2 broadcast_add_fusion
  55.1 0.4 fusion.27
  55.6 0.7 compare_select_fusion
  56.2 0.8 multiply_multiply_fusion.11
  57.0 0.2 pad_maximum_fusion.2
  57.2 0.0 copy-start.7
  57.2 0.1 broadcast_multiply_fusion.2
  57.4 0.1 pad_maximum_fusion.4
  57.5 0.0 copy-start.9
  57.5 0.5 broadcast_multiply_fusion.1
  58.0 0.0 copy-done.4
  58.0 0.0 copy-done.12
  58.1 0.0 copy-done.16
  58.1 4.4 %multiply_reduce_fusion.1 = f32[64,5,1024]{2,0,1:T(8,128)} fusion(f32[3,64,64,1]{2,1,3,0:T(8,128)S(1)} %copy-done.12, f32[3,1024]{1,0:T(4,128)S(1)} %copy-done.16, f32[5,64,1024]{2,1,0:T(8,128)S(1)} %copy-done.4), kind=kOutput, calls=%fused_computation.8 | convolution fusion | flops 756613120 | bytes 2682880 | tf_op jit(solution)/shard_map/dpq,vqe->dvpe/dot_general | solution.py:117
  62.4 0.0 copy-done.7
  62.5 1.0 copy.40
  63.5 1.8 mul.262
  65.2 0.0 collective-permute-done.1
  65.2 0.6 copy-done.15
  65.8 0.0 collective-permute-done
  65.8 3.8 %pad_maximum_fusion = f32[6272,96]{1,0:T(8,128)S(1)} fusion(f32[64,96]{1,0:T(8,128)} %copy-done.15, f32[64,96]{1,0:T(8,128)} %collective-permute-done, f32[6144,16]{1,0:T(8,128)} %bitcast.84, f32[6144,80]{1,0:T(8,128)} %copy.34), kind=kLoop, calls=%fused_computation.9 | loop fusion | flops 1806336 | bytes 4816896 | tf_op jit(solution)/shard_map/concatenate | solution.py:104
  69.6 20.9 %gather_fusion.1 = f32[6144,96]{1,0:T(8,128)} fusion(f32[6272,96]{1,0:T(8,128)S(1)} %pad_maximum_fusion, s32[6144]{0:T(1024)S(1)} %broadcast_clamp_fusion), kind=kCustom, calls=%fused_computation.1 | custom fusion | bytes 4743168 | tf_op jit(solution)/shard_map/jit(_take)/gather | solution.py:105
  90.5 4.8 %broadcast_select_fusion = f32[6144,96]{1,0:T(8,128)S(1)} fusion(f32[6144,96]{1,0:T(8,128)} %gather_fusion.1, pred[6144]{0:T(1024)(128)(4,1)S(1)} %compare_and_fusion.1), kind=kLoop, calls=%fused_computation.24 | loop fusion | flops 589824 | bytes 4724736 | tf_op jit(solution)/shard_map/jit(_take)/select_n | solution.py:105
  95.3 3.5 %broadcast_multiply_fusion = (f32[6144,16]{1,0:T(8,128)}, f32[6144,16]{1,0:T(8,128)}) fusion(f32[6144,96]{1,0:T(8,128)S(1)} %broadcast_select_fusion, f32[6,1024,16]{2,1,0:T(8,128)S(1)} %copy-done.1), kind=kLoop, calls=%fused_computation.23 | loop fusion | flops 491520 | bytes 1572864 | tf_op jit(solution)/shard_map/mul | solution.py:110
  98.8 2.1 copy.36
  100.9 3.4 %reshape.168 = f32[6,1024,16,5]{1,0,3,2:T(8,128)} reshape(f32[6144,80]{0,1:T(8,128)} %copy.36) | data formatting | bytes 3932160 | tf_op jit(solution)/shard_map/reshape | solution.py:106
  104.3 3.2 %copy.38 = f32[6,1024,16]{1,2,0:T(8,128)} copy(f32[6,1024,16]{2,1,0:T(8,128)} %bitcast.89) | data formatting | bytes 786432 | tf_op jit(solution)/shard_map/mul | solution.py:110
  107.5 3.0 %copy.35 = f32[6,1024,16]{1,2,0:T(8,128)} copy(f32[6,1024,16]{2,1,0:T(8,128)} %bitcast.88) | data formatting | bytes 786432 | tf_op jit(solution)/shard_map/mul | solution.py:110
  110.5 7.4 %multiply_add_fusion = (f32[5,64,1024]{2,1,0:T(8,128)}, f32[5,64,1024]{2,1,0:T(8,128)}) fusion(f32[5,64,1024]{2,1,0:T(8,128)S(1)} %copy-done.5, f32[64,16,6,1]{0,1,3,2:T(8,128)} %constant.156, f32[6,1024,16,5]{1,2,3,0:T(8,128)S(1)} %copy-done.3, f32[6,1024,16,5]{1,0,3,2:T(8,128)} %reshape.168, f32[6,1024,16]{1,2,0:T(8,128)} %copy.40, ...), kind=kOutput, calls=%fused_computation.30 | convolution fusion | flops 382238720 | bytes 10641408 | tf_op jit(solution)/shard_map/pqf,feqv->vpe/dot_general | solution.py:113
  117.9 1.8 copy.41
  119.7 34.7 %gather_fusion.2 = f32[8192,320]{1,0:T(8,128)} fusion(f32[1024,320]{1,0:T(8,128)S(1)} %copy.41, s32[8192]{0:T(1024)} %fusion.29), kind=kCustom, calls=%fused_computation.2 | custom fusion | bytes 21004288 | tf_op jit(solution)/shard_map/jit(_take)/gather | solution.py:131
  154.4 12.0 %copy.42 = f32[8192,320]{0,1:T(8,128)} copy(f32[8192,320]{1,0:T(8,128)} %gather_fusion.2) | data formatting | bytes 20971520 | tf_op jit(solution)/shard_map/jit(_take)/gather | solution.py:131
  166.4 5.7 %multiply_reduce_fusion = f32[8192,5]{0,1:T(8,128)S(1)} fusion(f32[8192,5,64]{0,2,1:T(8,128)} %bitcast.85, f32[8192,64]{0,1:T(8,128)S(1)} %bitcast.91, pred[8192]{0:T(1024)(128)(4,1)S(1)} %compare_and_fusion), kind=kLoop, calls=%fused_computation.5 | loop fusion | flops 7823360 | bytes 12754944
  172.1 2.6 %copy.53 = f32[8192,5]{1,0:T(8,128)} copy(f32[8192,5]{0,1:T(8,128)S(1)} %multiply_reduce_fusion) | data formatting | bytes 327680 | tf_op jit(solution)/shard_map/rvp,pr->rv/dot_general | solution.py:132
  174.7 24.5 %scatter_custom_fusion.1 = f32[16384,5]{1,0:T(8,128)} fusion(s32[8192]{0:T(1024)} %bitcast.106, f32[8192,5]{1,0:T(8,128)} %copy.53, f32[]{:T(128)} %constant.121.clone.1), kind=kCustom, calls=%fused_computation.6 | custom fusion | bytes 328192 | tf_op jit(solution)/shard_map/scatter | solution.py:163
  199.2 5.2 %copy.43 = f32[16,1024,5]{1,2,0:T(8,128)S(1)} copy(f32[16,1024,5]{2,1,0:T(8,128)} %bitcast.86) | data formatting | bytes 655360 | tf_op jit(solution)/shard_map/reshape | solution.py:164
  204.4 19.8 %all_to_all.5 = f32[16,5,1024]{2,1,0:T(8,128)S(1)} all-to-all(f32[16,5,1024]{2,1,0:T(8,128)S(1)} %bitcast.96), channel_id=1, replica_groups=mesh['valve'=8,'bulk'=16] {'bulk'}, dimensions={0} | all-to-all | bytes 655360 | tf_op jit(solution)/shard_map/all_to_all | solution.py:165
  224.2 0.8 copy.72
  (30 shorter events, 0.2 us)
Async XLA Ops:
  0.6 27.7 %copy-start.14 = (f32[16,6,64,1]{2,0,3,1:T(8,128)S(1)}, f32[16,6,64,1]{2,0,3,1:T(8,128)}, u32[]{:S(2)}) copy-start(f32[16,6,64,1]{2,0,3,1:T(8,128)} %constant.155) | copy-start | bytes 73732
  28.3 11.1 %copy-start = (f32[6,1024,16]{2,1,0:T(8,128)}, f32[6,1024,16]{2,1,0:T(8,128)S(1)}, u32[]{:S(2)}) copy-start(f32[6,1024,16]{2,1,0:T(8,128)S(1)} %copy.32) | copy-start | bytes 1179652
  32.3 3.7 %copy-start.2 = (f32[6,1024,16,5]{1,2,3,0:T(8,128)}, f32[6,1024,16,5]{1,2,3,0:T(8,128)S(1)}, u32[]{:S(2)}) copy-start(f32[6,1024,16,5]{1,2,3,0:T(8,128)S(1)} %convolution_bitcast_fusion) | copy-start | bytes 5898244
  39.4 9.1 %copy-start.10 = (s32[6,1024]{1,0:T(8,128)S(1)}, s32[6,1024]{1,0:T(8,128)}, u32[]{:S(2)}) copy-start(s32[6,1024]{1,0:T(8,128)} %param.15) | copy-start | bytes 73732
  39.4 9.1 %copy-start.11 = (s32[8192]{0:T(1024)S(1)}, s32[8192]{0:T(1024)}, u32[]{:S(2)}) copy-start(s32[8192]{0:T(1024)} %param.16) | copy-start | bytes 98308
  39.4 9.8 %copy-start.8 = (s32[8192,1]{0,1:T(1,128)S(1)}, s32[8192,1]{0,1:T(1,128)}, u32[]{:S(2)}) copy-start(s32[8192,1]{0,1:T(1,128)} %param.18) | copy-start | bytes 98308
  43.9 12.3 %copy-start.13 = (f32[3,8192]{1,0:T(4,128)S(1)}, f32[3,8192]{1,0:T(4,128)}, u32[]{:S(2)}) copy-start(f32[3,8192]{1,0:T(4,128)} %param.17) | copy-start | bytes 294916
  46.6 18.6 %collective-permute-start.1 = (f32[64,96]{1,0:T(8,128)S(1)}, f32[64,96]{1,0:T(8,128)S(1)}, u32[]{:S(2)}, u32[]{:S(2)}) collective-permute-start(f32[64,96]{1,0:T(8,128)S(1)} %get-tuple-element.17), channel_id=1, source_target_pairs={{16,0},{32,16},{48,32},{64,48},{80,64},{96,80},{112,96},{0,112},{1... | collective-permute-start | bytes 73736 | tf_op jit(solution)/shard_map/ppermute | solution.py:20
  47.3 18.5 %collective-permute-start = (f32[64,96]{1,0:T(8,128)S(1)}, f32[64,96]{1,0:T(8,128)}, u32[]{:S(2)}, u32[]{:S(2)}) collective-permute-start(f32[64,96]{1,0:T(8,128)S(1)} %get-tuple-element.16), channel_id=1, source_target_pairs={{0,16},{16,32},{32,48},{48,64},{64,80},{80,96},{96,112},{112,0},{1... | collective-permute-start | bytes 73736 | tf_op jit(solution)/shard_map/ppermute | solution.py:19
  54.9 3.1 %copy-start.4 = (f32[5,64,1024]{2,1,0:T(8,128)S(1)}, f32[5,64,1024]{2,1,0:T(8,128)}, u32[]{:S(2)}) copy-start(f32[5,64,1024]{2,1,0:T(8,128)} %param.11) | copy-start | bytes 3932164
  54.9 3.1 %copy-start.12 = (f32[3,64,64,1]{2,1,3,0:T(8,128)S(1)}, f32[3,64,64,1]{2,1,3,0:T(8,128)}, u32[]{:S(2)}) copy-start(f32[3,64,64,1]{2,1,3,0:T(8,128)} %constant.154) | copy-start | bytes 147460
  54.9 3.1 %copy-start.16 = (f32[3,1024]{1,0:T(4,128)S(1)}, f32[3,1024]{1,0:T(4,128)}, u32[]{:S(2)}) copy-start(f32[3,1024]{1,0:T(4,128)} %param.12) | copy-start | bytes 36868
  57.2 5.2 %copy-start.7 = (f32[16,6,1024]{2,1,0:T(8,128)S(1)}, f32[16,6,1024]{2,1,0:T(8,128)}, u32[]{:S(2)}) copy-start(f32[16,6,1024]{2,1,0:T(8,128)} %reshape.164) | copy-start | bytes 1179652
  57.5 5.9 %copy-start.9 = (f32[64,1024]{1,0:T(8,128)S(1)}, f32[64,1024]{1,0:T(8,128)}, u32[]{:S(2)}) copy-start(f32[64,1024]{1,0:T(8,128)} %param.13) | copy-start | bytes 786436
  65.2 0.6 copy-start.15
  90.5 4.8 %copy-start.1 = (f32[6,1024,16]{2,1,0:T(8,128)S(1)}, f32[6,1024,16]{2,1,0:T(8,128)}, u32[]{:S(2)}) copy-start(f32[6,1024,16]{2,1,0:T(8,128)} %copy-done) | copy-start | bytes 1179652
  104.3 6.2 %copy-start.3 = (f32[6,1024,16,5]{1,2,3,0:T(8,128)S(1)}, f32[6,1024,16,5]{1,2,3,0:T(8,128)}, u32[]{:S(2)}) copy-start(f32[6,1024,16,5]{1,2,3,0:T(8,128)} %copy-done.2) | copy-start | bytes 5898244
  104.3 6.2 %copy-start.5 = (f32[5,64,1024]{2,1,0:T(8,128)S(1)}, f32[5,64,1024]{2,1,0:T(8,128)}, u32[]{:S(2)}) copy-start(f32[5,64,1024]{2,1,0:T(8,128)} %param.11) | copy-start | bytes 3932164
  154.4 12.0 %copy-start.6 = (f32[64,8192]{1,0:T(8,128)S(1)}, f32[64,8192]{1,0:T(8,128)}, u32[]{:S(2)}) copy-start(f32[64,8192]{1,0:T(8,128)} %mul.262) | copy-start | bytes 6291460
